TPU v7x, 512 devices: a whole 4x4x16 slice. The times are simulated.
512 devices in a mesh: ctx: 64 (over z, y_lo, core), head: 8 (over x, y_hi).
Axes of the slice: x: 4, y: 4 (y_hi: 2, y_lo: 2; y = y_hi * 2 + y_lo), z: 16, core: 2. Of those that a mesh axis runs over, the one named last changes fastest.
Arguments:
- queries_nope: bfloat16 [4096, 8192], P('ctx', 'head'), may hold values from -4 to 4
- queries_rope: bfloat16 [4096, 4096], P('ctx', 'head'), may hold values from -128 to 128
- latents: bfloat16 [4096, 512], P('ctx'), may hold values from -8 to 8
- rope_keys: bfloat16 [4096, 64], P('ctx'), may hold values from -4 to 4
- positions: int32 [4096], P('ctx'), may hold values from 0 to 6143
- key_up: bfloat16 [512, 8192], P(None, 'head'), may hold values from -0.5 to 0.5
- value_up: bfloat16 [512, 8192], P(None, 'head'), may hold values from -0.25 to 0.25
- out_proj: bfloat16 [8192, 3584], P('head', 'ctx'), may hold values from -0.0625 to 0.0625
Outputs:
- attended: bfloat16 [4096, 3584], P('ctx', 'head')
All inputs are finite; a program needn't handle non-finite values.
Results may differ from a plain program's by a relative error of at most 0.014.
The roundings to bfloat16 on the way count: a program that leaves them out, or rounds other values in their place, can miss the bound.
Values may be sent and summed in bfloat16 or wider, within the bound.
No kernel may reach another device: no remote copies, remote signals or barrier semaphores. Data moves between devices by JAX's collectives and lax.ppermute only.
A program may use at most 64 MiB of HBM per device.

v0:
```python
import math
import jax
import jax.numpy as jnp
from jax import lax
from jax.sharding import PartitionSpec as P

LATENT = 512
ROPE = 64
NOPE = 128
VDIM = 128
masked_value = -1e30


def rope_tables(token_pos, width):
    half_width = width // 2
    freqs = jnp.exp(jnp.arange(half_width, dtype=jnp.float32) * (-2.0 * math.log(10000.0) / width))
    angle = token_pos.astype(jnp.float32)[:, None] * freqs[None, :]
    return (jnp.cos(angle), jnp.sin(angle))


def rotate(values, cosine, sine):
    half_width = values.shape[-1] // 2
    first_half = values[..., :half_width]
    second_half = values[..., half_width:]
    cos_part = cosine[:, None, :]
    sin_part = sine[:, None, :]
    return jnp.concatenate(
        [
            first_half * cos_part - second_half * sin_part,
            second_half * cos_part + first_half * sin_part,
        ],
        axis=-1,
    )


def attend(query_rows, query_index, keys, key_count):
    scale = 1.0 / math.sqrt(NOPE + ROPE)
    scores = jnp.einsum("rl,kl->rk", query_rows, keys, preferred_element_type=jnp.float32)
    key_index = lax.broadcasted_iota(jnp.int32, (1, key_count), 1)
    visible = key_index <= query_index[:, None]
    scores = jnp.where(visible, scores * scale, masked_value)
    peak = jnp.max(scores, axis=1)
    weights = jnp.where(visible, jnp.exp(scores - peak[:, None]), 0.0)
    totals = jnp.sum(weights, axis=1)
    summed = jnp.dot(
        weights.astype(jnp.bfloat16), keys[:, :LATENT], preferred_element_type=jnp.float32
    )
    return (summed / totals[:, None]).astype(jnp.bfloat16)


def upward(latent_out, value_up, token_count, head_count):
    head_out = jnp.einsum(
        "thl,lhd->thd",
        latent_out.reshape(token_count, head_count, LATENT),
        value_up.reshape(LATENT, head_count, VDIM),
        preferred_element_type=jnp.float32,
    )
    return head_out.astype(jnp.bfloat16).reshape(token_count, head_count * VDIM)


def body(queries_nope, queries_rope, latents, rope_keys, positions, key_up, value_up, out_proj):
    token_count = latents.shape[0]
    head_count = key_up.shape[1] // NOPE
    ctx_count = lax.axis_size("ctx")
    cosine, sine = rope_tables(positions, ROPE)
    rot_queries = rotate(
        queries_rope.astype(jnp.float32).reshape(token_count, head_count, ROPE), cosine, sine
    ).astype(jnp.bfloat16)
    rot_keys = rotate(rope_keys.astype(jnp.float32)[:, None, :], cosine, sine)[:, 0, :].astype(
        jnp.bfloat16
    )
    lat_queries = jnp.einsum(
        "thn,lhn->thl",
        queries_nope.reshape(token_count, head_count, NOPE),
        key_up.reshape(LATENT, head_count, NOPE),
        preferred_element_type=jnp.float32,
    ).astype(jnp.bfloat16)
    query_rows = jnp.concatenate([lat_queries, rot_queries], axis=-1).reshape(
        token_count * head_count, LATENT + ROPE
    )
    local_keys = jnp.concatenate([latents, rot_keys], axis=-1)
    keys = lax.all_gather(local_keys, "ctx", axis=0, tiled=True)
    first_token = lax.axis_index("ctx") * token_count
    query_index = jnp.repeat(first_token + jnp.arange(token_count, dtype=jnp.int32), head_count)
    latent_out = attend(query_rows, query_index, keys, token_count * ctx_count)
    head_out = upward(latent_out, value_up, token_count, head_count)
    partial_sums = jnp.dot(
        head_out,
        lax.all_gather(out_proj, "ctx", axis=1, tiled=True),
        preferred_element_type=jnp.float32,
    )
    return lax.psum_scatter(
        partial_sums.astype(jnp.bfloat16), "head", scatter_dimension=1, tiled=True
    )


def solution(mesh):
    in_specs = (
        P("ctx", "head"),
        P("ctx", "head"),
        P("ctx", None),
        P("ctx", None),
        P("ctx"),
        P(None, "head"),
        P(None, "head"),
        P("head", "ctx"),
    )
    out_specs = P("ctx", "head")
    return jax.shard_map(body, mesh=mesh, in_specs=in_specs, out_specs=out_specs, check_vma=False)
```

profile of v0, /device:TPU:2, one launch (start us, length us, event | category | flops | bytes accessed | tf_op | source)
XLA Modules:
  0.0 365.4 jit_solution(11109612518860116079)
XLA Ops:
  6.5 0.7 convert_element_type.33
  7.3 0.8 copy.34
  8.1 0.1 fusion.38
  8.3 0.1 copy.35
  8.4 1.5 pad_maximum_fusion.1
  9.9 0.7 all-gather.5.cloned.1.call-update
  10.7 1.0 reshape.133
  11.7 0.1 broadcast_in_dim.24
  11.7 0.1 le.16
  11.8 0.2 multiply_cosine_fusion
  12.0 0.1 fusion.44
  12.2 0.1 subtract_convert_fusion
  12.3 1.4 fusion.10
  13.7 0.1 pad_maximum_fusion
  13.8 126.6 %all-gather.3.cloned.1.call-done = bf16[4096,576]{1,0:T(8,128)(2,1)} async-done(((bf16[64,576]{1,0:T(8,128)(2,1)}), bf16[4096,576]{1,0:T(8,128)(2,1)}) %all-gather.3.cloned.1.call-update) | async-done | bytes 4718608 | tf_op jit(solution)/shard_map/all_gather | solution.py:82
  140.4 6.2 %fusion = (f32[512]{0:T(512)S(1)}, f32[512,4096]{1,0:T(8,128)S(1)}) fusion(s32[512]{0:T(512)S(1)} %le.16, bf16[4096,576]{1,0:T(8,128)(2,1)} %all-gather.3.cloned.1.call-done, bf16[64,8,576]{2,0,1:T(8,128)(2,1)S(1)} %pad_maximum_fusion), kind=kOutput, calls=%fused_computation.3 | convolution fusion | flops 2424307200 | bytes 13701120 | tf_op jit(solution)/shard_map/rl,kl->rk/dot_general | solution.py:38
  146.7 2.8 fusion.1
  149.5 2.7 fusion.20
  152.3 0.5 fusion.11
  152.7 114.3 %all-gather.5.cloned.1.call-done = bf16[1024,3584]{0,1:T(8,128)(2,1)} async-done(((bf16[1024,56]{0,1:T(8,128)(2,1)}), bf16[1024,3584]{0,1:T(8,128)(2,1)}) %all-gather.5.cloned.1.call-update) | async-done | bytes 7340048 | tf_op jit(solution)/shard_map/all_gather | solution.py:89
  267.0 5.4 %convolution_convert_fusion = bf16[64,3584]{1,0:T(8,128)(2,1)S(1)} fusion(bf16[1024,3584]{0,1:T(8,128)(2,1)} %all-gather.5.cloned.1.call-done, bf16[8,8,8,128]{3,2,1,0:T(8,128)(2,1)S(1)} %fusion.11), kind=kOutput, calls=%fused_computation.6 | convolution fusion | flops 469991424 | bytes 7929856 | tf_op jit(solution)/shard_map/dot_general | solution.py:87
  272.4 1.3 copy.39
  273.7 83.6 %reduce-scatter.4.cloned.1.call-done = bf16[448,64]{1,0:T(8,128)(2,1)} async-done(((bf16[3584,64]{1,0:T(8,128)(2,1)}), bf16[448,64]{1,0:T(8,128)(2,1)}) %reduce-scatter.4.cloned.1.call-update) | async-done | bytes 57360
  357.3 1.6 copy.40
  (15 shorter events, 0.2 us)
Async XLA Ops:
  6.5 5.8 %copy-start = (bf16[512,1024]{1,0:T(8,128)(2,1)S(1)}, bf16[512,1024]{1,0:T(8,128)(2,1)}, u32[]{:S(2)}) copy-start(bf16[512,1024]{1,0:T(8,128)(2,1)} %param.13) | copy-start | bytes 3145732
  6.5 133.9 %all-gather.3.cloned.1.call-start = ((), (), s32[]{:S(2)}) async-start(), calls=%async_computation.1 | async-start | bytes 5324800 | tf_op jit(solution)/shard_map/all_gather | solution.py:82
  9.9 257.1 %all-gather.5.cloned.1.call-start = ((), (), s32[]{:S(2)}) async-start(), calls=%async_computation.2 | async-start | bytes 7454720 | tf_op jit(solution)/shard_map/all_gather | solution.py:89
  10.6 346.6 %reduce-scatter.4.cloned.1.call-start = ((), (), s32[]{:S(2)}) async-start(), calls=%async_computation.3 | async-start | bytes 1032192
  146.6 2.9 copy-start.1
  149.5 2.8 copy-start.2
Sparse Core Ops, SparseCore 0:
  10.0 130.3 all-gather.2
  142.6 124.3 all-gather.4
  273.8 83.3 reduce-scatter.3
where the time goes:
time: 366 us; the launch traced here: 365 us
  waiting for transfers between devices  325 us (89%)
  matrix products  16.2 us (4%)
  between operations  13.2 us (4%)
  other arithmetic  5.66 us (2%)
  local copies, waits for them, and re-layouts  5.03 us (1%)
    all_gather x1, waiting for transfers between devices, body(): keys = lax.all_gather(local_keys, 'ctx', axis=0, tiled=True)  127 us
    all_gather x1, waiting for transfers between devices, body(): lax.all_gather(out_proj, 'ctx', axis=1, tiled=True)  114 us
    unnamed x4, waiting for transfers between devices  84.3 us
  transfers between devices with their start and end apart: 3, of which 3 were waited for; matrix products, arithmetic and copies ran while one was open for 4% of the time, Pallas kernels for 0%

commit v1 on v0

--- a/solution.py
+++ b/solution.py
@@ -79,7 +79,9 @@
         token_count * head_count, LATENT + ROPE
     )
     local_keys = jnp.concatenate([latents, rot_keys], axis=-1)
-    keys = lax.all_gather(local_keys, "ctx", axis=0, tiled=True)
+    keys = jnp.concatenate(
+        lax.all_to_all(jnp.stack([local_keys] * lax.axis_size("ctx")), "ctx", 0, 0), axis=0
+    )
     first_token = lax.axis_index("ctx") * token_count
     query_index = jnp.repeat(first_token + jnp.arange(token_count, dtype=jnp.int32), head_count)
     latent_out = attend(query_rows, query_index, keys, token_count * ctx_count)

time: 366 us -> 414 us (1.13)
  waiting for transfers between devices: 325 us -> 353 us
  starting transfers between devices: 0.08 us -> 17.4 us
    all_to_all x0 -> x1, waiting for transfers between devices: none -> 262 us  [body(): lax.all_to_all(jnp.stack([local_keys] * lax.axis_size('ctx')), 'ctx', 0, 0)]
    all_gather x1 -> x0, waiting for transfers between devices: 127 us -> none  [body(): keys = lax.all_gather(local_keys, 'ctx', axis=0, tiled=True)]
    all_gather x1, waiting for transfers between devices: 114 us -> 6.75 us  [body(): lax.all_gather(out_proj, 'ctx', axis=1, tiled=True)]
    all_to_all x0 -> x1, starting transfers between devices: none -> 17.3 us  [body(): lax.all_to_all(jnp.stack([local_keys] * lax.axis_size('ctx')), 'ctx', 0, 0)]
    unnamed x4 -> x3, waiting for transfers between devices: 84.3 us -> 84.4 us
where the time goes in v1:
time: 414 us
  waiting for transfers between devices  353 us (85%)
  matrix products  17.6 us (4%)
  starting transfers between devices  17.4 us (4%)
  between operations  13.6 us (3%)
  local copies, waits for them, and re-layouts  7.2 us (2%)
  other arithmetic  5.06 us (1%)
    all_to_all x1, waiting for transfers between devices, body(): lax.all_to_all(jnp.stack([local_keys] * lax.axis_size('ctx')), 'ctx', 0, 0)  262 us
    unnamed x3, waiting for transfers between devices  84.4 us
    all_to_all x1, starting transfers between devices, body(): lax.all_to_all(jnp.stack([local_keys] * lax.axis_size('ctx')), 'ctx', 0, 0)  17.3 us
  transfers between devices with their start and end apart: 3, of which 3 were waited for; matrix products, arithmetic and copies ran while one was open for 4% of the time, Pallas kernels for 0%

profile of v1, /device:TPU:2, one launch (start us, length us, event | category | flops | bytes accessed | tf_op | source)
XLA Modules:
  0.0 413.7 jit_solution(12847619730579834829)
XLA Ops:
  6.5 0.8 convert_element_type.33
  7.3 0.8 copy.34
  8.1 0.1 fusion.38
  8.4 0.9 pad_maximum_fusion.1
  9.3 3.0 stack.2
  12.3 17.3 %all-to-all-start = ((bf16[64,64,576]{2,1,0:T(8,128)(2,1)}), bf16[64,64,576]{2,1,0:T(8,128)(2,1)}, u32[]{:S(2)}, u32[]{:S(2)}) async-start(bf16[64,64,576]{2,1,0:T(8,128)(2,1)} %stack.2), calls=%async_computation | async-start | bytes 10485760 | tf_op jit(solution)/shard_map/all_to_all | solution.py:83
  29.7 0.7 all-gather.2.cloned.1.call-update
  30.4 0.1 reshape.139
  30.6 0.1 le.16
  30.7 0.2 multiply_cosine_fusion
  30.9 0.1 fusion.44
  31.1 0.1 subtract_convert_fusion
  31.2 0.5 fusion.10
  31.7 0.1 pad_maximum_fusion
  31.8 261.8 %all-to-all-done = bf16[64,64,576]{2,1,0:T(8,128)(2,1)} async-done(((bf16[64,64,576]{2,1,0:T(8,128)(2,1)}), bf16[64,64,576]{2,1,0:T(8,128)(2,1)}, u32[]{:S(2)}, u32[]{:S(2)}) %all-to-all-start) | async-done | bytes 4718624 | tf_op jit(solution)/shard_map/all_to_all | solution.py:83
  293.6 6.2 %fusion = (f32[512]{0:T(512)S(1)}, f32[512,4096]{1,0:T(8,128)S(1)}) fusion(s32[512]{0:T(512)S(1)} %le.16, bf16[4096,576]{1,0:T(8,128)(2,1)} %bitcast.5, bf16[64,8,576]{2,0,1:T(8,128)(2,1)S(1)} %pad_maximum_fusion), kind=kOutput, calls=%fused_computation.3 | convolution fusion | flops 2424307200 | bytes 13701120 | tf_op jit(solution)/shard_map/rl,kl->rk/dot_general | solution.py:38
  299.8 2.8 fusion.1
  302.6 5.0 %fusion.20 = bf16[64,8,512]{2,1,0:T(8,128)(2,1)S(1)} fusion(bf16[4096,576]{1,0:T(8,128)(2,1)} %bitcast.5, f32[512,4096]{1,0:T(8,128)S(1)} %get-tuple-element.14, f32[512]{0:T(512)S(1)} %get-tuple-element.13, s32[512]{0:T(512)S(1)} %le.16, f32[512]{0:T(512)S(1)} %fusion.1), kind=kOutput, calls=%fused_computation.22 | convolution fusion | flops 2160590848 | bytes 13113344 | tf_op jit(solution)/shard_map/dot_general | solution.py:45
  307.7 0.5 fusion.11
  308.1 6.8 %all-gather.2.cloned.1.call-done = bf16[1024,3584]{0,1:T(8,128)(2,1)} async-done(((bf16[1024,56]{0,1:T(8,128)(2,1)}), bf16[1024,3584]{0,1:T(8,128)(2,1)}) %all-gather.2.cloned.1.call-update) | async-done | bytes 7340048 | tf_op jit(solution)/shard_map/all_gather | solution.py:91
  314.9 5.4 %convolution_convert_fusion = bf16[64,3584]{1,0:T(8,128)(2,1)S(1)} fusion(bf16[1024,3584]{0,1:T(8,128)(2,1)} %all-gather.2.cloned.1.call-done, bf16[8,8,8,128]{3,2,1,0:T(8,128)(2,1)S(1)} %fusion.11), kind=kOutput, calls=%fused_computation.6 | convolution fusion | flops 469991424 | bytes 7929856 | tf_op jit(solution)/shard_map/dot_general | solution.py:89
  320.3 1.3 copy.39
  321.6 83.7 %reduce-scatter.4.cloned.1.call-done = bf16[448,64]{1,0:T(8,128)(2,1)} async-done(((bf16[3584,64]{1,0:T(8,128)(2,1)}), bf16[448,64]{1,0:T(8,128)(2,1)}) %reduce-scatter.4.cloned.1.call-update) | async-done | bytes 57360
  405.3 1.6 copy.40
  (17 shorter events, 0.3 us)
Async XLA Ops:
  6.5 24.6 %copy-start = (bf16[512,1024]{1,0:T(8,128)(2,1)S(1)}, bf16[512,1024]{1,0:T(8,128)(2,1)}, u32[]{:S(2)}) copy-start(bf16[512,1024]{1,0:T(8,128)(2,1)} %param.13) | copy-start | bytes 3145732
  6.5 23.9 %copy-start.1 = (bf16[64,512]{1,0:T(8,128)(2,1)S(1)}, bf16[64,512]{1,0:T(8,128)(2,1)}, u32[]{:S(2)}) copy-start(bf16[64,512]{1,0:T(8,128)(2,1)} %param.9) | copy-start | bytes 196612
  9.3 21.9 %copy-start.3 = (bf16[64,1024]{1,0:T(8,128)(2,1)S(1)}, bf16[64,1024]{1,0:T(8,128)(2,1)}, u32[]{:S(2)}) copy-start(bf16[64,1024]{1,0:T(8,128)(2,1)} %param.8) | copy-start | bytes 393220
  12.3 281.3 %all-to-all-start = ((bf16[64,64,576]{2,1,0:T(8,128)(2,1)}), bf16[64,64,576]{2,1,0:T(8,128)(2,1)}, u32[]{:S(2)}, u32[]{:S(2)}) async-start(bf16[64,64,576]{2,1,0:T(8,128)(2,1)} %stack.2), calls=%async_computation | async-start | bytes 10485760 | tf_op jit(solution)/shard_map/all_to_all | solution.py:83
  29.6 285.3 %all-gather.2.cloned.1.call-start = ((), (), s32[]{:S(2)}) async-start(), calls=%async_computation.2 | async-start | bytes 7454720 | tf_op jit(solution)/shard_map/all_gather | solution.py:91
  30.4 374.9 %reduce-scatter.4.cloned.1.call-start = ((), (), s32[]{:S(2)}) async-start(), calls=%async_computation.3 | async-start | bytes 1032192
  302.6 5.1 %copy-start.2 = (bf16[512,1024]{1,0:T(8,128)(2,1)S(1)}, bf16[512,1024]{1,0:T(8,128)(2,1)}, u32[]{:S(2)}) copy-start(bf16[512,1024]{1,0:T(8,128)(2,1)} %param.14) | copy-start | bytes 3145732
Sparse Core Ops, SparseCore 0:
  32.6 282.2 all-gather.1
  321.7 83.5 reduce-scatter.3
